TPU v7x, 256 devices: a whole 4x4x8 slice. The times are simulated.
256 devices in a mesh: seq: 128 (over x, y, z_lo, core), dp: 2 (over z_hi).
Axes of the slice: x: 4, y: 4, z: 8 (z_hi: 2, z_lo: 4; z = z_hi * 4 + z_lo), core: 2. Of those that a mesh axis runs over, the one named last changes fastest.
Arguments:
- inputs: bfloat16 [2, 256, 256, 512], P('dp', 'seq'), may hold values from -6 to 6
- gate: bfloat16 [2, 256, 256, 512], P('dp', 'seq'), may hold values from -6 to 6
- kernel: bfloat16 [256, 256, 512], P(None, 'seq'), may hold values from -6 to 6
- first_blocks: bfloat16 [256, 256, 256], P('seq'), may hold values from -0.375 to 0.375
- second_blocks: bfloat16 [256, 256, 256], P('seq'), may hold values from -0.375 to 0.375
- cotangent: bfloat16 [2, 256, 256, 512], P('dp', 'seq'), may hold values from -6 to 6
Outputs:
- mixed: bfloat16 [2, 256, 256, 512], P('dp', 'seq')
- grad_inputs: bfloat16 [2, 256, 256, 512], P('dp', 'seq')
- grad_gate: bfloat16 [2, 256, 256, 512], P('dp', 'seq')
- grad_kernel: float32 [256, 256, 512], P(None, 'seq')
All inputs are finite; a program needn't handle non-finite values.
Results may differ from a plain program's by a relative error of at most 0.007.
Values may be sent and summed in bfloat16 or wider, within the bound.
No kernel may reach another device: no remote copies, remote signals or barrier semaphores. Data moves between devices by JAX's collectives and lax.ppermute only.
A program may use at most 64 MiB of HBM per device.

v0:
```python
import jax
import jax.numpy as jnp
from jax import lax
from jax.sharding import PartitionSpec as P


def shards(inputs, gate, kernel, first_blocks, second_blocks, cotangent):
    f32 = jnp.float32
    bf16 = jnp.bfloat16
    gate32 = gate.astype(f32)
    cot = cotangent.astype(f32)
    d_result = (cot * gate32).astype(bf16)

    def spread(rows):
        return jnp.einsum("rij,srjd->srid", first_blocks, rows, preferred_element_type=f32).astype(
            bf16
        )

    def mix_columns(piece):
        return jnp.einsum("cqr,srcd->sqcd", second_blocks, piece, preferred_element_type=f32)

    def unmix_columns(scaled):
        return jnp.einsum(
            "cqr,sqcd->srcd", second_blocks, scaled, preferred_element_type=f32
        ).astype(bf16)

    def finish_rows(piece):
        return jnp.einsum("rij,srid->srjd", first_blocks, piece, preferred_element_type=f32)

    second = mix_columns(
        lax.all_to_all(spread(inputs), "seq", split_axis=2, concat_axis=1, tiled=True)
    )
    hidden = (second * kernel).astype(bf16)
    result = finish_rows(
        lax.all_to_all(unmix_columns(hidden), "seq", split_axis=1, concat_axis=2, tiled=True)
    )
    d_hidden = mix_columns(
        lax.all_to_all(spread(d_result), "seq", split_axis=2, concat_axis=1, tiled=True)
    )
    d_second = (d_hidden * kernel).astype(bf16)
    d_inputs = finish_rows(
        lax.all_to_all(unmix_columns(d_second), "seq", split_axis=1, concat_axis=2, tiled=True)
    )
    mixed = (result * gate32).astype(bf16)
    grad_gate = (cot * result).astype(bf16)
    grad_inputs = d_inputs.astype(bf16)
    grad_kernel = lax.psum(jnp.sum(d_hidden * second, axis=0), "dp")
    return (mixed, grad_inputs, grad_gate, grad_kernel)


def solution(mesh):
    placed = (
        P("dp", "seq", None, None),
        P("dp", "seq", None, None),
        P(None, "seq", None),
        P("seq", None, None),
        P("seq", None, None),
        P("dp", "seq", None, None),
    )
    return jax.shard_map(
        shards,
        mesh=mesh,
        in_specs=placed,
        out_specs=(
            P("dp", "seq", None, None),
            P("dp", "seq", None, None),
            P("dp", "seq", None, None),
            P(None, "seq", None),
        ),
        check_vma=False,
    )
```

profile of v0, /device:TPU:1, one launch (start us, length us, event | category | flops | bytes accessed | tf_op | source)
XLA Modules:
  0.0 193.4 jit_solution(5639259495040109000)
XLA Ops:
  7.2 0.0 copy-start
  7.2 1.0 copy-done
  8.2 1.3 fusion
  9.5 1.2 copy.43
  10.7 14.0 %all-to-all-start = ((bf16[1,2,256,512]{3,1,0,2:T(2,128)(2,1)}), bf16[1,2,256,512]{3,1,0,2:T(2,128)(2,1)S(1)}, u32[]{:S(2)}, u32[]{:S(2)}) async-start(bf16[1,2,256,512]{3,1,0,2:T(2,128)(2,1)} %copy.43), calls=%async_computation | async-start | bytes 1048576 | tf_op jit(solution)/shard_map/all_to_all | solution.py:31
  24.7 0.0 copy-start.11
  24.7 0.2 copy.51
  24.9 0.8 copy-done.11
  25.7 0.2 copy.50
  25.9 0.7 copy-done.6
  26.7 0.3 fusion.2
  27.0 0.4 copy-done.1
  27.5 1.2 copy.52
  28.6 14.2 %all-to-all-done = bf16[1,2,256,512]{3,1,0,2:T(2,128)(2,1)S(1)} async-done(((bf16[1,2,256,512]{3,1,0,2:T(2,128)(2,1)}), bf16[1,2,256,512]{3,1,0,2:T(2,128)(2,1)S(1)}, u32[]{:S(2)}, u32[]{:S(2)}) %all-to-all-start) | async-done | bytes 524320 | tf_op jit(solution)/shard_map/all_to_all | solution.py:31
  42.8 0.8 copy-done.8
  43.6 6.9 %all-to-all-start.2 = ((bf16[1,2,256,512]{3,1,0,2:T(2,128)(2,1)}), bf16[1,2,256,512]{3,1,0,2:T(2,128)(2,1)S(1)}, u32[]{:S(2)}, u32[]{:S(2)}) async-start(bf16[1,2,256,512]{3,1,0,2:T(2,128)(2,1)} %copy.52), calls=%async_computation.2 | async-start | bytes 1048576 | tf_op jit(solution)/shard_map/all_to_all | solution.py:38
  50.6 0.0 copy-start.9
  50.6 0.5 copy.46
  51.1 0.5 copy-done.9
  51.6 0.4 copy.44
  52.0 0.5 copy-done.5
  52.6 0.3 convolution_bitcast_fusion.2
  52.9 1.1 fusion.1
  54.0 2.0 %copy.47 = bf16[1,256,2,512]{3,2,0,1:T(2,128)(2,1)} copy(bf16[1,256,2,512]{1,3,2,0:T(8,128)(2,1)} %fusion.1) | data formatting | bytes 1048576 | tf_op jit(solution)/shard_map/convert_element_type | solution.py:25
  56.0 12.7 %all-to-all-done.2 = bf16[1,2,256,512]{3,1,0,2:T(2,128)(2,1)S(1)} async-done(((bf16[1,2,256,512]{3,1,0,2:T(2,128)(2,1)}), bf16[1,2,256,512]{3,1,0,2:T(2,128)(2,1)S(1)}, u32[]{:S(2)}, u32[]{:S(2)}) %all-to-all-start.2) | async-done | bytes 524320 | tf_op jit(solution)/shard_map/all_to_all | solution.py:38
  68.7 7.5 %all-to-all-start.1 = ((bf16[1,256,2,512]{3,2,0,1:T(2,128)(2,1)}), bf16[1,256,2,512]{3,2,0,1:T(2,128)(2,1)}, u32[]{:S(2)}, u32[]{:S(2)}) async-start(bf16[1,256,2,512]{3,2,0,1:T(2,128)(2,1)} %copy.47), calls=%async_computation.1 | async-start | bytes 1048576 | tf_op jit(solution)/shard_map/all_to_all | solution.py:35
  76.2 0.4 copy.53
  76.6 0.3 convolution_bitcast_fusion
  77.0 0.7 copy-done.4
  77.7 1.1 fusion.3
  78.8 2.0 %copy.55 = bf16[1,256,2,512]{3,2,0,1:T(2,128)(2,1)} copy(bf16[1,256,2,512]{1,3,2,0:T(8,128)(2,1)} %fusion.3) | data formatting | bytes 1048576 | tf_op jit(solution)/shard_map/convert_element_type | solution.py:25
  80.8 13.4 %all-to-all-done.1 = bf16[1,256,2,512]{3,2,0,1:T(2,128)(2,1)} async-done(((bf16[1,256,2,512]{3,2,0,1:T(2,128)(2,1)}), bf16[1,256,2,512]{3,2,0,1:T(2,128)(2,1)}, u32[]{:S(2)}, u32[]{:S(2)}) %all-to-all-start.1) | async-done | bytes 524320 | tf_op jit(solution)/shard_map/all_to_all | solution.py:35
  94.1 7.7 %all-to-all-start.3 = ((bf16[1,256,2,512]{3,2,0,1:T(2,128)(2,1)}), bf16[1,256,2,512]{3,2,0,1:T(2,128)(2,1)}, u32[]{:S(2)}, u32[]{:S(2)}) async-start(bf16[1,256,2,512]{3,2,0,1:T(2,128)(2,1)} %copy.55), calls=%async_computation.3 | async-start | bytes 1048576 | tf_op jit(solution)/shard_map/all_to_all | solution.py:42
  101.8 0.0 all-reduce.2.cloned.1.call-start
  101.8 1.1 multiply_bitcast_fusion
  102.9 0.0 all-reduce.2.cloned.1.call-update
  103.0 0.0 copy-start.2
  103.0 0.0 copy-start.7
  103.0 1.5 copy.48
  104.5 0.4 fusion.7
  104.9 1.0 copy.58
  105.9 13.8 %all-to-all-done.3 = bf16[1,256,2,512]{3,2,0,1:T(2,128)(2,1)} async-done(((bf16[1,256,2,512]{3,2,0,1:T(2,128)(2,1)}), bf16[1,256,2,512]{3,2,0,1:T(2,128)(2,1)}, u32[]{:S(2)}, u32[]{:S(2)}) %all-to-all-start.3) | async-done | bytes 524320 | tf_op jit(solution)/shard_map/all_to_all | solution.py:42
  119.7 1.5 copy.56
  121.1 0.3 fusion.4
  121.5 1.0 copy.59
  122.5 1.0 copy.60
  123.5 60.8 %all-reduce.2.cloned.1.call-done = f32[256,2,512]{0,2,1:T(8,128)} async-done(((f32[256,2,512]{0,2,1:T(8,128)}), f32[256,2,512]{0,2,1:T(8,128)}) %all-reduce.2.cloned.1.call-update) | async-done | bytes 1048592 | tf_op jit(solution)/shard_map/psum | solution.py:47
  184.3 2.2 %copy.61 = f32[256,2,512]{2,1,0:T(2,128)} copy(f32[256,2,512]{0,2,1:T(8,128)} %all-reduce.2.cloned.1.call-done) | data formatting | bytes 2097152
  (13 shorter events, 0.0 us)
Async XLA Ops:
  7.2 1.0 copy-start
  10.7 14.0 %copy-start.10 = (bf16[1,2,256,512]{3,2,1,0:T(8,128)(2,1)S(1)}, bf16[1,2,256,512]{3,2,1,0:T(8,128)(2,1)}, u32[]{:S(2)}) copy-start(bf16[1,2,256,512]{3,2,1,0:T(8,128)(2,1)} %param.11) | copy-start | bytes 1572868
  10.7 32.1 %all-to-all-start = ((bf16[1,2,256,512]{3,1,0,2:T(2,128)(2,1)}), bf16[1,2,256,512]{3,1,0,2:T(2,128)(2,1)S(1)}, u32[]{:S(2)}, u32[]{:S(2)}) async-start(bf16[1,2,256,512]{3,1,0,2:T(2,128)(2,1)} %copy.43), calls=%async_computation | async-start | bytes 1048576 | tf_op jit(solution)/shard_map/all_to_all | solution.py:31
  24.7 1.0 copy-start.11
  25.7 0.9 copy-start.6
  26.7 0.8 copy-start.1
  28.6 21.9 %copy-start.12 = (bf16[256,2,512]{2,1,0:T(2,128)(2,1)S(1)}, bf16[256,2,512]{2,1,0:T(2,128)(2,1)}, u32[]{:S(2)}) copy-start(bf16[256,2,512]{2,1,0:T(2,128)(2,1)} %param.8) | copy-start | bytes 1572868
  42.8 0.8 copy-start.8
  43.6 25.1 %all-to-all-start.2 = ((bf16[1,2,256,512]{3,1,0,2:T(2,128)(2,1)}), bf16[1,2,256,512]{3,1,0,2:T(2,128)(2,1)S(1)}, u32[]{:S(2)}, u32[]{:S(2)}) async-start(bf16[1,2,256,512]{3,1,0,2:T(2,128)(2,1)} %copy.52), calls=%async_computation.2 | async-start | bytes 1048576 | tf_op jit(solution)/shard_map/all_to_all | solution.py:38
  50.6 1.0 copy-start.9
  51.1 1.8 copy-start.3
  51.6 0.9 copy-start.5
  68.7 25.4 %all-to-all-start.1 = ((bf16[1,256,2,512]{3,2,0,1:T(2,128)(2,1)}), bf16[1,256,2,512]{3,2,0,1:T(2,128)(2,1)}, u32[]{:S(2)}, u32[]{:S(2)}) async-start(bf16[1,256,2,512]{3,2,0,1:T(2,128)(2,1)} %copy.47), calls=%async_computation.1 | async-start | bytes 1048576 | tf_op jit(solution)/shard_map/all_to_all | solution.py:35
  76.6 1.0 copy-start.4
  94.1 25.6 %all-to-all-start.3 = ((bf16[1,256,2,512]{3,2,0,1:T(2,128)(2,1)}), bf16[1,256,2,512]{3,2,0,1:T(2,128)(2,1)}, u32[]{:S(2)}, u32[]{:S(2)}) async-start(bf16[1,256,2,512]{3,2,0,1:T(2,128)(2,1)} %copy.55), calls=%async_computation.3 | async-start | bytes 1048576 | tf_op jit(solution)/shard_map/all_to_all | solution.py:42
  101.8 82.6 %all-reduce.2.cloned.1.call-start = ((), (), s32[]{:S(2)}) async-start(), calls=%async_computation.4 | async-start | bytes 2097152 | tf_op jit(solution)/shard_map/psum | solution.py:47
  103.0 1.6 copy-start.2
  103.0 1.6 copy-start.7
Sparse Core Ops, SparseCore 0:
  105.8 78.5 all-reduce.1
where the time goes:
time: 194 us; the launch traced here: 193 us
  waiting for transfers between devices  115 us (59%)
  starting transfers between devices  36.1 us (19%)
  local copies, waits for them, and re-layouts  21.9 us (11%)
  between operations  14.2 us (7%)
  matrix products  5.23 us (3%)
    psum x1, waiting for transfers between devices, shards(): grad_kernel = lax.psum(jnp.sum(d_hidden * second, axis=0), 'dp')  60.8 us
    all_to_all x1, waiting for transfers between devices, shards(): lax.all_to_all(spread(inputs), 'seq', split_axis=2, concat_axis=1, tiled=...  14.2 us
    all_to_all x1, starting transfers between devices, shards(): lax.all_to_all(spread(inputs), 'seq', split_axis=2, concat_axis=1, tiled=...  14 us
    all_to_all x1, waiting for transfers between devices, shards(): lax.all_to_all(unmix_columns(d_second), 'seq', split_axis=1, concat_axis=...  13.8 us
    all_to_all x1, waiting for transfers between devices, shards(): lax.all_to_all(unmix_columns(hidden), 'seq', split_axis=1, concat_axis=2,...  13.4 us
    all_to_all x1, waiting for transfers between devices, shards(): lax.all_to_all(spread(d_result), 'seq', split_axis=2, concat_axis=1, tile...  12.7 us
    unnamed x33, local copies, waits for them, and re-layouts  11.8 us
    all_to_all x1, starting transfers between devices, shards(): lax.all_to_all(unmix_columns(d_second), 'seq', split_axis=1, concat_axis=...  7.66 us
  transfers between devices with their start and end apart: 5, of which 5 were waited for; matrix products, arithmetic and copies ran while one was open for 9% of the time, Pallas kernels for 0%

commit v1 on v0

--- a/solution.py
+++ b/solution.py
@@ -44,7 +44,7 @@
     mixed = (result * gate32).astype(bf16)
     grad_gate = (cot * result).astype(bf16)
     grad_inputs = d_inputs.astype(bf16)
-    grad_kernel = lax.psum(jnp.sum(d_hidden * second, axis=0), "dp")
+    grad_kernel = jnp.sum(lax.all_gather(jnp.sum(d_hidden * second, axis=0), "dp"), axis=0)
     return (mixed, grad_inputs, grad_gate, grad_kernel)
 
 

time: 194 us -> 179 us (0.923)
  waiting for transfers between devices: 115 us -> 96 us
  matrix products: 5.23 us -> 9.57 us
    psum x1 -> x0, waiting for transfers between devices: 60.8 us -> none  [shards(): grad_kernel = lax.psum(jnp.sum(d_hidden * second, axis=0), 'dp')]
    all_to_all x1, waiting for transfers between devices: 13.8 us -> 55.3 us  [shards(): lax.all_to_all(unmix_columns(d_second), 'seq', split_axis=1, concat_axis=...]
    all_to_all x1, starting transfers between devices: 14 us -> 6.93 us  [shards(): lax.all_to_all(spread(inputs), 'seq', split_axis=2, concat_axis=1, tiled=...]
    all_to_all x1, starting transfers between devices: 6.93 us -> 13.8 us  [shards(): lax.all_to_all(spread(d_result), 'seq', split_axis=2, concat_axis=1, tile...]
    all_to_all x1, waiting for transfers between devices: 13.4 us -> 8.39 us  [shards(): lax.all_to_all(unmix_columns(hidden), 'seq', split_axis=1, concat_axis=2,...]
    all_to_all x1, waiting for transfers between devices: 12.7 us -> 16.6 us  [shards(): lax.all_to_all(spread(d_result), 'seq', split_axis=2, concat_axis=1, tile...]
    dot_general x2, matrix products: 0.69 us -> 4.07 us  [mix_columns(): jnp.einsum('cqr,srcd->sqcd', second_blocks, piece, preferred_element_type...]
    unnamed x33 -> x13, local copies, waits for them, and re-layouts: 11.8 us -> 8.66 us
  transfers between devices with their start and end apart: 5 -> 5, of which waited for: 5 -> 4; matrix products, arithmetic and copies ran while one was open for 9% -> 11% of each run, Pallas kernels for 0% -> 0%
where the time goes in v1:
time: 179 us; the launch traced here: 178 us
  waiting for transfers between devices  96 us (54%)
  starting transfers between devices  35.2 us (20%)
  local copies, waits for them, and re-layouts  21.1 us (12%)
  between operations  14.2 us (8%)
  matrix products  9.57 us (5%)
  other arithmetic  1.9 us (1%)
    all_to_all x1, waiting for transfers between devices, shards(): lax.all_to_all(unmix_columns(d_second), 'seq', split_axis=1, concat_axis=...  55.3 us
    all_to_all x1, waiting for transfers between devices, shards(): lax.all_to_all(spread(d_result), 'seq', split_axis=2, concat_axis=1, tile...  16.6 us
    all_to_all x1, waiting for transfers between devices, shards(): lax.all_to_all(spread(inputs), 'seq', split_axis=2, concat_axis=1, tiled=...  15.6 us
    all_to_all x1, starting transfers between devices, shards(): lax.all_to_all(spread(d_result), 'seq', split_axis=2, concat_axis=1, tile...  13.8 us
    unnamed x13, local copies, waits for them, and re-layouts  8.66 us
    all_to_all x1, waiting for transfers between devices, shards(): lax.all_to_all(unmix_columns(hidden), 'seq', split_axis=1, concat_axis=2,...  8.39 us
    all_to_all x1, starting transfers between devices, shards(): lax.all_to_all(unmix_columns(hidden), 'seq', split_axis=1, concat_axis=2,...  7.48 us
    all_to_all x1, starting transfers between devices, shards(): lax.all_to_all(spread(inputs), 'seq', split_axis=2, concat_axis=1, tiled=...  6.93 us
  transfers between devices with their start and end apart: 5, of which 4 were waited for; matrix products, arithmetic and copies ran while one was open for 11% of the time, Pallas kernels for 0%

profile of v1, /device:TPU:1, one launch (start us, length us, event | category | flops | bytes accessed | tf_op | source)
XLA Modules:
  0.0 178.0 jit_solution(5469219848976568522)
XLA Ops:
  7.2 0.0 copy-start
  7.2 0.0 copy-start.1
  7.2 1.3 copy.48
  8.5 1.2 copy.49
  9.8 0.0 copy-done.1
  9.8 0.3 fusion.2
  10.1 1.2 copy.50
  11.3 13.8 %all-to-all-start.2 = ((bf16[1,2,256,512]{3,1,0,2:T(2,128)(2,1)}), bf16[1,2,256,512]{3,1,0,2:T(2,128)(2,1)S(1)}, u32[]{:S(2)}, u32[]{:S(2)}) async-start(bf16[1,2,256,512]{3,1,0,2:T(2,128)(2,1)} %copy.50), calls=%async_computation.2 | async-start | bytes 1048576 | tf_op jit(solution)/shard_map/all_to_all | solution.py:38
  25.1 0.0 copy-done
  25.1 0.3 fusion
  25.5 1.2 copy.41
  26.7 16.6 %all-to-all-done.2 = bf16[1,2,256,512]{3,1,0,2:T(2,128)(2,1)S(1)} async-done(((bf16[1,2,256,512]{3,1,0,2:T(2,128)(2,1)}), bf16[1,2,256,512]{3,1,0,2:T(2,128)(2,1)S(1)}, u32[]{:S(2)}, u32[]{:S(2)}) %all-to-all-start.2) | async-done | bytes 524320 | tf_op jit(solution)/shard_map/all_to_all | solution.py:38
  43.3 6.9 %all-to-all-start = ((bf16[1,2,256,512]{3,1,0,2:T(2,128)(2,1)}), bf16[1,2,256,512]{3,1,0,2:T(2,128)(2,1)S(1)}, u32[]{:S(2)}, u32[]{:S(2)}) async-start(bf16[1,2,256,512]{3,1,0,2:T(2,128)(2,1)} %copy.41), calls=%async_computation | async-start | bytes 1048576 | tf_op jit(solution)/shard_map/all_to_all | solution.py:31
  50.2 1.3 copy.44
  51.5 1.2 copy.51
  52.7 15.6 %all-to-all-done = bf16[1,2,256,512]{3,1,0,2:T(2,128)(2,1)S(1)} async-done(((bf16[1,2,256,512]{3,1,0,2:T(2,128)(2,1)}), bf16[1,2,256,512]{3,1,0,2:T(2,128)(2,1)S(1)}, u32[]{:S(2)}, u32[]{:S(2)}) %all-to-all-start) | async-done | bytes 524320 | tf_op jit(solution)/shard_map/all_to_all | solution.py:31
  68.4 0.4 copy.42
  68.8 1.3 convolution_bitcast_fusion.2
  70.1 2.0 %fusion.1 = bf16[1,256,2,512]{1,3,2,0:T(8,128)(2,1)} fusion(bf16[2,256,256]{2,1,0:T(8,128)(2,1)} %param.10, f32[1,256,2,512]{1,3,2,0:T(8,128)S(1)} %convolution_bitcast_fusion.2, bf16[256,2,512]{0,2,1:T(8,128)(2,1)S(1)} %copy.44), kind=kOutput, calls=%fused_computation.14 | convolution fusion | flops 135266304 | bytes 2359296 | tf_op jit(solution)/shard_map/cqr,sqcd->srcd/dot_general | solution.py:23
  72.1 2.0 %copy.45 = bf16[1,256,2,512]{3,2,0,1:T(2,128)(2,1)} copy(bf16[1,256,2,512]{1,3,2,0:T(8,128)(2,1)} %fusion.1) | data formatting | bytes 1048576 | tf_op jit(solution)/shard_map/convert_element_type | solution.py:25
  74.2 7.5 %all-to-all-start.1 = ((bf16[1,256,2,512]{3,2,0,1:T(2,128)(2,1)}), bf16[1,256,2,512]{3,2,0,1:T(2,128)(2,1)}, u32[]{:S(2)}, u32[]{:S(2)}) async-start(bf16[1,256,2,512]{3,2,0,1:T(2,128)(2,1)} %copy.45), calls=%async_computation.1 | async-start | bytes 1048576 | tf_op jit(solution)/shard_map/all_to_all | solution.py:35
  81.6 0.0 all-gather.2.cloned.1.call-start
  81.7 2.8 %fusion.23 = (f32[1,256,2,512]{1,3,2,0:T(8,128)}, f32[1,256,2,512]{1,3,2,0:T(8,128)}) fusion(f32[1,256,2,512]{1,3,2,0:T(8,128)S(1)} %convolution_bitcast_fusion.2, bf16[2,256,256]{2,1,0:T(8,128)(2,1)} %param.10, bf16[256,2,512]{2,1,0:T(2,128)(2,1)} %bitcast.78), kind=kOutput, calls=%fused_computation.33 | convolution fusion | flops 134479872 | bytes 3932160 | tf_op jit(solution)/shard_map/cqr,srcd->sqcd/dot_general | solution.py:20
  84.5 0.0 copy-start.2
  84.5 2.6 %copy.56 = f32[1,256,2,512]{3,1,2,0:T(8,128)} copy(f32[1,256,2,512]{1,3,2,0:T(8,128)} %get-tuple-element.18) | data formatting | bytes 2097152 | tf_op jit(solution)/shard_map/mul | solution.py:47
  87.1 0.0 all-gather.2.cloned.1.call-update
  87.1 0.0 copy-done.2
  87.1 2.0 %fusion.3 = bf16[1,256,2,512]{1,3,2,0:T(8,128)(2,1)} fusion(bf16[2,256,256]{2,1,0:T(8,128)(2,1)} %param.10, f32[1,256,2,512]{1,3,2,0:T(8,128)S(1)} %copy-done.2, bf16[256,2,512]{0,2,1:T(8,128)(2,1)S(1)} %copy.44), kind=kOutput, calls=%fused_computation.16 | convolution fusion | flops 135266304 | bytes 2359296 | tf_op jit(solution)/shard_map/cqr,sqcd->srcd/dot_general | solution.py:23
  89.2 2.0 %copy.53 = bf16[1,256,2,512]{3,2,0,1:T(2,128)(2,1)} copy(bf16[1,256,2,512]{1,3,2,0:T(8,128)(2,1)} %fusion.3) | data formatting | bytes 1048576 | tf_op jit(solution)/shard_map/convert_element_type | solution.py:25
  91.2 8.4 %all-to-all-done.1 = bf16[1,256,2,512]{3,2,0,1:T(2,128)(2,1)} async-done(((bf16[1,256,2,512]{3,2,0,1:T(2,128)(2,1)}), bf16[1,256,2,512]{3,2,0,1:T(2,128)(2,1)}, u32[]{:S(2)}, u32[]{:S(2)}) %all-to-all-start.1) | async-done | bytes 524320 | tf_op jit(solution)/shard_map/all_to_all | solution.py:35
  99.6 6.9 %all-to-all-start.3 = ((bf16[1,256,2,512]{3,2,0,1:T(2,128)(2,1)}), bf16[1,256,2,512]{3,2,0,1:T(2,128)(2,1)S(1)}, u32[]{:S(2)}, u32[]{:S(2)}) async-start(bf16[1,256,2,512]{3,2,0,1:T(2,128)(2,1)} %copy.53), calls=%async_computation.3 | async-start | bytes 1048576 | tf_op jit(solution)/shard_map/all_to_all | solution.py:42
  106.5 1.5 copy.46
  108.0 0.4 fusion.7
  108.3 1.0 copy.60
  109.3 1.0 copy.58
  110.4 55.3 %all-to-all-done.3 = bf16[1,256,2,512]{3,2,0,1:T(2,128)(2,1)S(1)} async-done(((bf16[1,256,2,512]{3,2,0,1:T(2,128)(2,1)}), bf16[1,256,2,512]{3,2,0,1:T(2,128)(2,1)S(1)}, u32[]{:S(2)}, u32[]{:S(2)}) %all-to-all-start.3) | async-done | bytes 524320 | tf_op jit(solution)/shard_map/all_to_all | solution.py:42
  165.7 0.4 copy.54
  166.1 0.3 fusion.4
  166.5 1.0 copy.59
  167.5 0.0 all-gather.2.cloned.1.call-done
  167.5 1.9 %reduce_sum.8 = f32[256,2,512]{2,0,1:T(8,128)S(1)} reduce(f32[2,256,2,512]{3,1,2,0:T(8,128)} %all-gather.2.cloned.1.call-done, f32[]{:T(128)} %constant.0.clone.1), dimensions={0}, to_apply=%region_0.0 | reduce | flops 262144 | bytes 3145732 | tf_op jit(solution)/shard_map/reduce_sum | solution.py:47
  169.4 1.8 %copy.61 = f32[256,2,512]{2,1,0:T(2,128)} copy(f32[256,2,512]{2,0,1:T(8,128)S(1)} %reduce_sum.8) | data formatting | bytes 2097152
Async XLA Ops:
  7.2 18.0 %copy-start = (bf16[1,2,256,512]{3,2,1,0:T(8,128)(2,1)S(1)}, bf16[1,2,256,512]{3,2,1,0:T(8,128)(2,1)}, u32[]{:S(2)}) copy-start(bf16[1,2,256,512]{3,2,1,0:T(8,128)(2,1)} %param.6) | copy-start | bytes 1572868
  7.2 2.6 %copy-start.1 = (bf16[2,256,256]{2,1,0:T(8,128)(2,1)S(1)}, bf16[2,256,256]{2,1,0:T(8,128)(2,1)}, u32[]{:S(2)}) copy-start(bf16[2,256,256]{2,1,0:T(8,128)(2,1)} %param.9) | copy-start | bytes 786436
  11.3 32.0 %all-to-all-start.2 = ((bf16[1,2,256,512]{3,1,0,2:T(2,128)(2,1)}), bf16[1,2,256,512]{3,1,0,2:T(2,128)(2,1)S(1)}, u32[]{:S(2)}, u32[]{:S(2)}) async-start(bf16[1,2,256,512]{3,1,0,2:T(2,128)(2,1)} %copy.50), calls=%async_computation.2 | async-start | bytes 1048576 | tf_op jit(solution)/shard_map/all_to_all | solution.py:38
  43.3 25.1 %all-to-all-start = ((bf16[1,2,256,512]{3,1,0,2:T(2,128)(2,1)}), bf16[1,2,256,512]{3,1,0,2:T(2,128)(2,1)S(1)}, u32[]{:S(2)}, u32[]{:S(2)}) async-start(bf16[1,2,256,512]{3,1,0,2:T(2,128)(2,1)} %copy.41), calls=%async_computation | async-start | bytes 1048576 | tf_op jit(solution)/shard_map/all_to_all | solution.py:31
  74.2 25.4 %all-to-all-start.1 = ((bf16[1,256,2,512]{3,2,0,1:T(2,128)(2,1)}), bf16[1,256,2,512]{3,2,0,1:T(2,128)(2,1)}, u32[]{:S(2)}, u32[]{:S(2)}) async-start(bf16[1,256,2,512]{3,2,0,1:T(2,128)(2,1)} %copy.45), calls=%async_computation.1 | async-start | bytes 1048576 | tf_op jit(solution)/shard_map/all_to_all | solution.py:35
  81.6 85.8 %all-gather.2.cloned.1.call-start = ((), (), s32[]{:S(2)}) async-start(), calls=%async_computation.4 | async-start | bytes 3145728 | tf_op jit(solution)/shard_map/all_gather | solution.py:47
  84.5 2.6 %copy-start.2 = (f32[1,256,2,512]{1,3,2,0:T(8,128)S(1)}, f32[1,256,2,512]{1,3,2,0:T(8,128)}, u32[]{:S(2)}) copy-start(f32[1,256,2,512]{1,3,2,0:T(8,128)} %get-tuple-element.19) | copy-start | bytes 3145732
  99.6 66.1 %all-to-all-start.3 = ((bf16[1,256,2,512]{3,2,0,1:T(2,128)(2,1)}), bf16[1,256,2,512]{3,2,0,1:T(2,128)(2,1)S(1)}, u32[]{:S(2)}, u32[]{:S(2)}) async-start(bf16[1,256,2,512]{3,2,0,1:T(2,128)(2,1)} %copy.53), calls=%async_computation.3 | async-start | bytes 1048576 | tf_op jit(solution)/shard_map/all_to_all | solution.py:42
Sparse Core Ops, SparseCore 0:
  87.2 73.6 all-gather.1
